TPU v7x, 32 devices: a whole 2x2x4 slice. The times are simulated.
32 devices in a mesh: blk: 4 (over y, x), group: 8 (over z, core).
Axes of the slice: x: 2, y: 2, z: 4, core: 2. Of those that a mesh axis runs over, the one named last changes fastest.
Arguments:
- picture_vector_list: bfloat16 [8, 1024, 768], P('group', 'blk'), may hold values from -0.25 to 0.25
- caption_latent_matrix: bfloat16 [8, 1024, 3072], P('group', 'blk'), may hold values from -6 to 6
- linear_map_matrix: bfloat16 [3072, 768], P('group'), may hold values from -0.109375 to 0.109375
- target_match_index: int32 [8, 1024], P('group', 'blk'), may hold values from 0 to 1023, each once within a row
- sharpness_factor: float32 [1], replicated, may hold values from 24 to 40
- offset_term: float32 [1], replicated, may hold values from -6 to -5
Outputs:
- row_loss: float32 [8, 1024], P('group', 'blk')
- image_grad: bfloat16 [8, 1024, 768], P('group', 'blk')
- projection_grad: float32 [3072, 768], P(('blk', 'group'))
Inputs may be any that keep to these rules, and one draw needn't show every extreme that they name: `target_match_index`: each data group's row of positives is a permutation of 0 to 1023.
All inputs are finite; a program needn't handle non-finite values.
Results may differ from a plain program's by a relative error of at most 0.015.
Values may be sent and summed in bfloat16 or wider, within the bound.
No kernel may reach another device: no remote copies, remote signals or barrier semaphores. Data moves between devices by JAX's collectives and lax.ppermute only.
A program may use at most 64 MiB of HBM per device.

v0:
```python
import jax
import jax.numpy as jnp
from jax import lax
from jax.sharding import PartitionSpec as P

epsilon = 1e-06


def passed_along(value, axis, steps):
    count = lax.axis_size(axis)
    pairs = [(source, (source + steps) % count) for source in range(count)]
    return lax.ppermute(value, axis, pairs)


def body(
    picture_vector_list,
    caption_latent_matrix,
    linear_map_matrix,
    target_match_index,
    sharpness_factor,
    offset_term,
):
    image_rows = picture_vector_list[0]
    hidden_rows = caption_latent_matrix[0]
    label_rows = target_match_index[0]
    row_count = image_rows.shape[0]
    feature_dim = image_rows.shape[1]
    blocks = lax.axis_size("blk")
    my_index = lax.axis_index("blk")
    multiplier_amount = sharpness_factor[0]
    offset_value = offset_term[0]
    columns = hidden_rows
    projected = jnp.dot(
        columns,
        lax.all_gather(linear_map_matrix, "group", axis=0, tiled=True),
        preferred_element_type=jnp.float32,
    )
    text_scale = lax.rsqrt(jnp.sum(projected * projected, axis=1, keepdims=True) + epsilon)
    text_dir = projected * text_scale
    text_unit = text_dir.astype(jnp.bfloat16)
    image_float = image_rows.astype(jnp.float32)
    image_scale = lax.rsqrt(jnp.sum(image_float * image_float, axis=1, keepdims=True) + epsilon)
    image_dir = image_float * image_scale
    image_unit = image_dir.astype(jnp.bfloat16)

    def signed_logits(image_tile_rows, label_block, text_block, column_start):
        columns = column_start + jnp.arange(text_block.shape[0], dtype=jnp.int32)
        pair_sign = jnp.where(label_block[:, None] == columns[None, :], 1.0, -1.0).astype(
            jnp.float32
        )
        pair_scores = lax.dot_general(
            image_tile_rows,
            text_block,
            (((1,), (1,)), ((), ())),
            preferred_element_type=jnp.float32,
        )
        return (multiplier_amount * pair_scores + offset_value, pair_sign)

    def weights_of(logits, pair_sign):
        return (-pair_sign * jax.nn.sigmoid(-pair_sign * logits) * multiplier_amount).astype(
            jnp.bfloat16
        )

    image_unit_grad = jnp.zeros((row_count, feature_dim), jnp.float32)
    loss_local = jnp.zeros((row_count,), jnp.float32)
    text_block = text_unit
    for step_index in range(blocks):
        source = (my_index - step_index) % blocks
        logits, pair_sign = signed_logits(image_unit, label_rows, text_block, source * row_count)
        loss_local = loss_local + -jnp.sum(jax.nn.log_sigmoid(pair_sign * logits), axis=1)
        pair_weight = weights_of(logits, pair_sign)
        image_unit_grad = image_unit_grad + jnp.dot(
            pair_weight, text_block, preferred_element_type=jnp.float32
        )
        if step_index + 1 < blocks:
            text_block = passed_along(text_block, "blk", 1)
    own_start = my_index * row_count
    image_piece = lax.all_gather(image_unit, "blk", axis=0, tiled=True)
    label_piece = lax.all_gather(label_rows, "blk", axis=0, tiled=True)
    logits, pair_sign = signed_logits(image_piece, label_piece, text_unit, own_start)
    pair_weight = weights_of(logits, pair_sign)
    text_unit_grad = lax.dot_general(
        pair_weight, image_piece, (((0,), (0,)), ((), ())), preferred_element_type=jnp.float32
    )
    image_grad = (
        image_scale
        * (
            image_unit_grad
            - image_dir * jnp.sum(image_dir * image_unit_grad, axis=1, keepdims=True)
        )
    ).astype(jnp.bfloat16)
    projection_output_gradient = (
        text_scale
        * (text_unit_grad - text_dir * jnp.sum(text_dir * text_unit_grad, axis=1, keepdims=True))
    ).astype(jnp.bfloat16)
    columns = hidden_rows
    projection_grad = lax.psum_scatter(
        lax.dot_general(
            columns,
            projection_output_gradient,
            (((0,), (0,)), ((), ())),
            preferred_element_type=jnp.float32,
        ),
        ("blk", "group"),
        scatter_dimension=0,
        tiled=True,
    )
    return (loss_local[None], image_grad[None], projection_grad)


def solution(mesh):
    return jax.shard_map(
        body,
        mesh=mesh,
        in_specs=(
            P("group", "blk", None),
            P("group", "blk", None),
            P("group", None),
            P("group", "blk"),
            P(),
            P(),
        ),
        out_specs=(P("group", "blk"), P("group", "blk", None), P(("blk", "group"), None)),
        check_vma=False,
    )
```

profile of v0, /device:TPU:0, one launch (start us, length us, event | category | flops | bytes accessed | tf_op | source)
XLA Modules:
  0.0 257.5 jit_solution(9647050227928517033)
XLA Ops:
  7.2 0.0 copy-start
  7.2 0.0 copy-start.3
  7.2 0.0 all-gather.4.cloned.1.call-start
  7.2 0.7 all-gather.4.cloned.1.call-update
  7.9 0.0 all-gather.6.cloned.1.call-start
  8.0 1.2 fusion.27
  9.1 1.9 fusion.22
  11.0 0.0 all-gather.6.cloned.1.call-update
  11.0 0.0 reduce-scatter.4.cloned.1.call-start
  12.4 0.0 copy-done.3
  12.4 10.1 %all-gather = s32[1,1024]{1,0:T(1,128)} all-gather(s32[1,256]{1,0:T(1,128)S(1)} %copy-done.3), channel_id=2, replica_groups=mesh['blk'=4,'group'=8] {'blk'}, dimensions={1}, use_global_device_ids=true | all-gather | bytes 5120 | tf_op jit(solution)/shard_map/all_gather | solution.py:79
  22.5 0.6 iota_add_fusion
  23.0 41.1 %all-gather.4.cloned.1.call-done = bf16[3072,768]{1,0:T(8,128)(2,1)} async-done(((bf16[384,768]{1,0:T(8,128)(2,1)}), bf16[3072,768]{1,0:T(8,128)(2,1)}) %all-gather.4.cloned.1.call-update) | async-done | bytes 4718608 | tf_op jit(solution)/shard_map/all_gather | solution.py:35
  64.1 0.0 copy-done
  64.1 3.8 %multiply_reduce_fusion.1 = (f32[256]{0:T(256)S(1)}, f32[256,768]{1,0:T(8,128)S(1)}) fusion(bf16[3072,768]{1,0:T(8,128)(2,1)} %all-gather.4.cloned.1.call-done, bf16[1,256,3072]{2,1,0:T(8,128)(2,1)S(1)} %copy-done), kind=kOutput, calls=%fused_computation.41 | convolution fusion | flops 1208352512 | bytes 7078912 | tf_op jit(solution)/shard_map/dot_general | solution.py:33
  67.9 0.1 multiply_convert_fusion.1
  68.0 28.3 %all-gather.6.cloned.1.call-done = bf16[1024,768]{1,0:T(8,128)(2,1)} async-done(((bf16[256,768]{1,0:T(8,128)(2,1)}), bf16[1024,768]{1,0:T(8,128)(2,1)}) %all-gather.6.cloned.1.call-update) | async-done | bytes 1572880 | tf_op jit(solution)/shard_map/all_gather | solution.py:78
  96.3 3.9 %multiply_reduce_fusion = (f32[256]{0:T(256)S(1)}, f32[256,768]{1,0:T(8,128)S(1)}) fusion(f32[256,768]{1,0:T(8,128)S(1)} %get-tuple-element.14, f32[256]{0:T(256)S(1)} %add_rsqrt_fusion, bf16[1024,768]{1,0:T(8,128)(2,1)} %all-gather.6.cloned.1.call-done, bf16[256,768]{1,0:T(8,128)(2,1)S(1)} %multiply_convert_fusion.1, f32[]{:T(128)} %bitcast.49, ...), kind=kOutput, calls=%fused_computation.40 | convolution fusion | flops 809041664 | bytes 3546120 | tf_op jit(solution)/shard_map/dot_general | solution.py:82
  100.2 5.3 %convolution_bitcast_fusion = f32[3072,768]{0,1:T(8,128)} fusion(bf16[1,256,3072]{2,1,0:T(8,128)(2,1)S(1)} %copy-done, f32[256,768]{1,0:T(8,128)S(1)} %get-tuple-element.19, f32[256,768]{1,0:T(8,128)S(1)} %get-tuple-element.14, f32[256]{0:T(256)S(1)} %get-tuple-element.18, f32[256]{0:T(256)S(1)} %add_rsqrt_fusion), kind=kOutput, calls=%fused_computation | convolution fusion | flops 1208942592 | bytes 12584960 | tf_op jit(solution)/shard_map/dot_general | solution.py:98
  105.5 9.6 %copy.11 = f32[3072,768]{1,0:T(8,128)} copy(f32[3072,768]{0,1:T(8,128)} %convolution_bitcast_fusion) | data formatting | bytes 18874368
  115.1 0.0 copy-start.1
  115.1 0.0 reduce-scatter.4.cloned.1.call-update
  115.2 1.5 collective-permute-start
  116.7 10.3 %collective-permute-done = bf16[256,768]{1,0:T(8,128)(2,1)S(1)} collective-permute-done((bf16[256,768]{1,0:T(8,128)(2,1)S(1)}, bf16[256,768]{1,0:T(8,128)(2,1)S(1)}, u32[]{:S(2)}, u32[]{:S(2)}) %collective-permute-start) | collective-permute-done | bytes 393248 | tf_op jit(solution)/shard_map/ppermute | solution.py:12
  127.0 0.6 collective-permute-start.1
  127.5 0.0 copy-done.1
  127.5 0.3 fusion.12
  127.8 10.0 %collective-permute-done.1 = bf16[256,768]{1,0:T(8,128)(2,1)S(1)} collective-permute-done((bf16[256,768]{1,0:T(8,128)(2,1)S(1)}, bf16[256,768]{1,0:T(8,128)(2,1)S(1)}, u32[]{:S(2)}, u32[]{:S(2)}) %collective-permute-start.1) | collective-permute-done | bytes 393248 | tf_op jit(solution)/shard_map/ppermute | solution.py:12
  137.8 0.0 collective-permute-start.2
  137.8 0.4 fusion.77
  138.3 0.3 fusion.14
  138.6 9.2 %collective-permute-done.2 = bf16[256,768]{1,0:T(8,128)(2,1)S(1)} collective-permute-done((bf16[256,768]{1,0:T(8,128)(2,1)S(1)}, bf16[256,768]{1,0:T(8,128)(2,1)S(1)}, u32[]{:S(2)}, u32[]{:S(2)}) %collective-permute-start.2) | collective-permute-done | bytes 393248 | tf_op jit(solution)/shard_map/ppermute | solution.py:12
  147.8 0.3 fusion.15
  148.1 0.9 fusion.70
  149.0 0.6 add_add_fusion
  149.6 0.4 convolution_add_fusion.2
  150.0 0.0 copy-start.2
  150.0 0.4 convolution_add_fusion.1
  150.5 0.5 copy-done.2
  151.0 0.5 fusion.23
  151.6 1.0 fusion.34
  152.5 98.5 %reduce-scatter.4.cloned.1.call-done = f32[96,768]{1,0:T(8,128)} async-done(((f32[3072,768]{1,0:T(8,128)}), f32[96,768]{1,0:T(8,128)}) %reduce-scatter.4.cloned.1.call-update) | async-done | bytes 294928
  (4 shorter events, 0.0 us)
Async XLA Ops:
  7.2 56.9 %copy-start = (bf16[1,256,3072]{2,1,0:T(8,128)(2,1)S(1)}, bf16[1,256,3072]{2,1,0:T(8,128)(2,1)}, u32[]{:S(2)}) copy-start(bf16[1,256,3072]{2,1,0:T(8,128)(2,1)} %param.7) | copy-start | bytes 4718596
  7.2 5.2 %copy-start.3 = (s32[1,256]{1,0:T(1,128)S(1)}, s32[1,256]{1,0:T(1,128)}, u32[]{:S(2)}) copy-start(s32[1,256]{1,0:T(1,128)} %param.9) | copy-start | bytes 3076
  7.2 56.9 %all-gather.4.cloned.1.call-start = ((), (), s32[]{:S(2)}) async-start(), calls=%async_computation.1 | async-start | bytes 5308416 | tf_op jit(solution)/shard_map/all_gather | solution.py:35
  7.9 88.4 %all-gather.6.cloned.1.call-start = ((), (), s32[]{:S(2)}) async-start(), calls=%async_computation.2 | async-start | bytes 1966080 | tf_op jit(solution)/shard_map/all_gather | solution.py:78
  11.0 240.0 %reduce-scatter.4.cloned.1.call-start = ((), (), s32[]{:S(2)}) async-start(), calls=%async_computation.3 | async-start | bytes 9732096
  115.1 12.4 %copy-start.1 = (bf16[256,768]{1,0:T(8,128)(2,1)S(1)}, bf16[256,768]{1,0:T(8,128)(2,1)}, u32[]{:S(2)}) copy-start(bf16[256,768]{1,0:T(8,128)(2,1)} %fusion.22) | copy-start | bytes 1179652
  115.2 11.8 %collective-permute-start = (bf16[256,768]{1,0:T(8,128)(2,1)S(1)}, bf16[256,768]{1,0:T(8,128)(2,1)S(1)}, u32[]{:S(2)}, u32[]{:S(2)}) collective-permute-start(bf16[256,768]{1,0:T(8,128)(2,1)S(1)} %multiply_convert_fusion.1), channel_id=1, source_target_pairs={{0,8},{8,16},{16,24},{24,0},{1,9},{9,17},{17,25},{25,1},{2,10},{10... | collective-permute-start | bytes 1179656 | tf_op jit(solution)/shard_map/ppermute | solution.py:12
  127.0 10.9 %collective-permute-start.1 = (bf16[256,768]{1,0:T(8,128)(2,1)S(1)}, bf16[256,768]{1,0:T(8,128)(2,1)S(1)}, u32[]{:S(2)}, u32[]{:S(2)}) collective-permute-start(bf16[256,768]{1,0:T(8,128)(2,1)S(1)} %collective-permute-done), channel_id=1, source_target_pairs={{0,8},{8,16},{16,24},{24,0},{1,9},{9,17},{17,25},{25,1},{2,10},{10... | collective-permute-start | bytes 1179656 | tf_op jit(solution)/shard_map/ppermute | solution.py:12
  137.8 10.0 %collective-permute-start.2 = (bf16[256,768]{1,0:T(8,128)(2,1)S(1)}, bf16[256,768]{1,0:T(8,128)(2,1)S(1)}, u32[]{:S(2)}, u32[]{:S(2)}) collective-permute-start(bf16[256,768]{1,0:T(8,128)(2,1)S(1)} %collective-permute-done.1), channel_id=1, source_target_pairs={{0,8},{8,16},{16,24},{24,0},{1,9},{9,17},{17,25},{25,1},{2,10},{10... | collective-permute-start | bytes 1179656 | tf_op jit(solution)/shard_map/ppermute | solution.py:12
  150.0 1.0 copy-start.2
Sparse Core Ops, SparseCore 0:
  9.7 54.3 all-gather.3
  66.5 29.7 all-gather.5
  115.3 135.6 reduce-scatter.3
where the time goes:
time: 258 us
  waiting for transfers between devices  198 us (77%)
  matrix products  16.6 us (6%)
  between operations  15.1 us (6%)
  local copies, waits for them, and re-layouts  10.2 us (4%)
  blocking collectives  10.1 us (4%)
  other arithmetic  5.28 us (2%)
    unnamed x4, waiting for transfers between devices  99.2 us
    all_gather x1, waiting for transfers between devices, body(): lax.all_gather(linear_map_matrix, 'group', axis=0, tiled=True)  41.1 us
    ppermute x3, waiting for transfers between devices, passed_along(): return lax.ppermute(value, axis, pairs)  29.5 us
    all_gather x1, waiting for transfers between devices, body(): image_piece = lax.all_gather(image_unit, 'blk', axis=0, tiled=True)  28.3 us
    unnamed x9, local copies, waits for them, and re-layouts  10.2 us
    all_gather x1, blocking collectives, body(): label_piece = lax.all_gather(label_rows, 'blk', axis=0, tiled=True)  10.1 us
    dot_general x1, matrix products, body(): lax.dot_general(columns, projection_output_gradient, (((0,), (0,)), ((),...  5.27 us
  transfers between devices with their start and end apart: 6, of which 6 were waited for; matrix products, arithmetic and copies ran while one was open for 5% of the time, Pallas kernels for 0%

commit v1 on v0

--- a/solution.py
+++ b/solution.py
@@ -4,6 +4,28 @@
 from jax.sharding import PartitionSpec as P
 
 epsilon = 1e-06
+
+
+def laid_out(blocks, dim):
+    shape = list(blocks.shape[1:])
+    shape[dim] *= blocks.shape[0]
+    return jnp.moveaxis(blocks, 0, dim).reshape(shape)
+
+
+def gather_around(x, axis, dim):
+    devices = lax.axis_size(axis)
+    pairs = [(i, (i + 1) % devices) for i in range(devices)]
+    back = [(b, a) for a, b in pairs]
+    lower, upper = ([], [])
+    for hop in range(devices - 1):
+        if hop % 2 == 0:
+            lower.append(lax.ppermute(lower[-1] if lower else x, axis, pairs))
+        else:
+            upper.append(lax.ppermute(upper[-1] if upper else x, axis, back))
+    tiles = jnp.stack([*lower[::-1], x, *upper])
+    shift = lax.axis_index(axis) - len(lower)
+    tiles = tiles[(jnp.arange(devices) - shift) % devices]
+    return laid_out(tiles, dim)
 
 
 def passed_along(value, axis, steps):
@@ -31,9 +53,7 @@
     offset_value = offset_term[0]
     columns = hidden_rows
     projected = jnp.dot(
-        columns,
-        lax.all_gather(linear_map_matrix, "group", axis=0, tiled=True),
-        preferred_element_type=jnp.float32,
+        columns, gather_around(linear_map_matrix, "group", 0), preferred_element_type=jnp.float32
     )
     text_scale = lax.rsqrt(jnp.sum(projected * projected, axis=1, keepdims=True) + epsilon)
     text_dir = projected * text_scale

time: 258 us -> 250 us (0.969)
  waiting for transfers between devices: 198 us -> 166 us
  local copies, waits for them, and re-layouts: 10.2 us -> 26.1 us
  starting transfers between devices: 2.2 us -> 11.6 us
    all_gather x1 -> x0, waiting for transfers between devices: 41.1 us -> none  [body(): lax.all_gather(linear_map_matrix, 'group', axis=0, tiled=True)]
    ppermute x0 -> x7, waiting for transfers between devices: none -> 37.6 us  [the longest x4 37.6 us: gather_around(): lower.append(lax.ppermute(lower[-1] if lower else x, axis, pairs))]
    all_gather x1, waiting for transfers between devices: 28.3 us -> 0.02 us  [body(): image_piece = lax.all_gather(image_unit, 'blk', axis=0, tiled=True)]
    unnamed x9 -> x18, local copies, waits for them, and re-layouts: 10.2 us -> 20 us
    ppermute x0 -> x7, starting transfers between devices: none -> 9.5 us  [the longest x3 8.99 us: gather_around(): upper.append(lax.ppermute(upper[-1] if upper else x, axis, back))]
    gather x0 -> x1, local copies, waits for them, and re-layouts: none -> 5.35 us  [gather_around(): tiles = tiles[(jnp.arange(devices) - shift) % devices]]
    unnamed x4 -> x3, waiting for transfers between devices: 99.2 us -> 98.9 us
  transfers between devices with their start and end apart: 6 -> 12, of which waited for: 6 -> 7; matrix products, arithmetic and copies ran while one was open for 5% -> 12% of each run, Pallas kernels for 0% -> 0%
where the time goes in v1:
time: 250 us; the launch traced here: 249 us
  waiting for transfers between devices  166 us (66%)
  local copies, waits for them, and re-layouts  26.1 us (10%)
  matrix products  16.5 us (7%)
  between operations  15.5 us (6%)
  starting transfers between devices  11.6 us (5%)
  blocking collectives  8.28 us (3%)
  other arithmetic  5.25 us (2%)
    unnamed x3, waiting for transfers between devices  98.9 us
    ppermute x4, waiting for transfers between devices, gather_around(): lower.append(lax.ppermute(lower[-1] if lower else x, axis, pairs))  37.6 us
    ppermute x3, waiting for transfers between devices, passed_along(): return lax.ppermute(value, axis, pairs)  29.4 us
    unnamed x18, local copies, waits for them, and re-layouts  20 us
    ppermute x3, starting transfers between devices, gather_around(): upper.append(lax.ppermute(upper[-1] if upper else x, axis, back))  8.99 us
    all_gather x1, blocking collectives, body(): label_piece = lax.all_gather(label_rows, 'blk', axis=0, tiled=True)  8.28 us
    gather x1, local copies, waits for them, and re-layouts, gather_around(): tiles = tiles[(jnp.arange(devices) - shift) % devices]  5.35 us
    dot_general x1, matrix products, body(): lax.dot_general(columns, projection_output_gradient, (((0,), (0,)), ((),...  5.09 us
  transfers between devices with their start and end apart: 12, of which 7 were waited for; matrix products, arithmetic and copies ran while one was open for 12% of the time, Pallas kernels for 0%

profile of v1, /device:TPU:0, one launch (start us, length us, event | category | flops | bytes accessed | tf_op | source)
XLA Modules:
  0.0 249.2 jit_solution(14052421555127993131)
XLA Ops:
  7.2 0.0 copy-start
  7.2 0.0 copy-start.3
  7.2 0.0 all-gather.3.cloned.1.call-start
  7.2 0.5 collective-permute-start
  7.7 11.8 %collective-permute-done = bf16[384,768]{1,0:T(8,128)(2,1)S(1)} collective-permute-done((bf16[384,768]{1,0:T(8,128)(2,1)}, bf16[384,768]{1,0:T(8,128)(2,1)S(1)}, u32[]{:S(2)}, u32[]{:S(2)}) %collective-permute-start) | collective-permute-done | bytes 589856 | tf_op jit(solution)/shard_map/ppermute | solution.py:22
  19.6 0.0 collective-permute-start.1
  19.6 3.5 %collective-permute-start.4 = (bf16[384,768]{1,0:T(8,128)(2,1)}, bf16[384,768]{1,0:T(8,128)(2,1)S(1)}, u32[]{:S(2)}, u32[]{:S(2)}) collective-permute-start(bf16[384,768]{1,0:T(8,128)(2,1)} %param.8), channel_id=1, source_target_pairs={{1,0},{2,1},{3,2},{4,3},{5,4},{6,5},{7,6},{0,7},{9,8},{10,9},{11,1... | collective-permute-start | bytes 1769480 | tf_op jit(solution)/shard_map/ppermute | solution.py:24
  23.1 13.1 %collective-permute-done.1 = bf16[384,768]{1,0:T(8,128)(2,1)} collective-permute-done((bf16[384,768]{1,0:T(8,128)(2,1)S(1)}, bf16[384,768]{1,0:T(8,128)(2,1)}, u32[]{:S(2)}, u32[]{:S(2)}) %collective-permute-start.1) | collective-permute-done | bytes 589856 | tf_op jit(solution)/shard_map/ppermute | solution.py:22
  36.2 0.0 collective-permute-start.2
  36.2 1.2 fusion.27
  37.3 0.0 collective-permute-done.4
  37.3 3.6 %collective-permute-start.5 = (bf16[384,768]{1,0:T(8,128)(2,1)S(1)}, bf16[384,768]{1,0:T(8,128)(2,1)}, u32[]{:S(2)}, u32[]{:S(2)}) collective-permute-start(bf16[384,768]{1,0:T(8,128)(2,1)S(1)} %collective-permute-done.4), channel_id=1, source_target_pairs={{1,0},{2,1},{3,2},{4,3},{5,4},{6,5},{7,6},{0,7},{9,8},{10,9},{11,1... | collective-permute-start | bytes 1769480 | tf_op jit(solution)/shard_map/ppermute | solution.py:24
  40.9 12.7 %collective-permute-done.2 = bf16[384,768]{1,0:T(8,128)(2,1)} collective-permute-done((bf16[384,768]{1,0:T(8,128)(2,1)}, bf16[384,768]{1,0:T(8,128)(2,1)}, u32[]{:S(2)}, u32[]{:S(2)}) %collective-permute-start.2) | collective-permute-done | bytes 589856 | tf_op jit(solution)/shard_map/ppermute | solution.py:22
  53.6 0.0 collective-permute-start.3
  53.6 1.9 fusion.22
  55.5 0.0 all-gather.3.cloned.1.call-update
  55.5 0.0 reduce-scatter.4.cloned.1.call-start
  56.9 8.3 %all-gather = s32[1,1024]{1,0:T(1,128)S(1)} all-gather(s32[1,256]{1,0:T(1,128)} %param.9), channel_id=2, replica_groups=mesh['blk'=4,'group'=8] {'blk'}, dimensions={1}, use_global_device_ids=true | all-gather | bytes 5120 | tf_op jit(solution)/shard_map/all_gather | solution.py:99
  65.2 0.6 iota_add_fusion
  65.7 0.0 collective-permute-done.5
  65.7 1.9 collective-permute-start.6
  67.6 0.0 collective-permute-done.3
  67.6 1.9 bitcast_dynamic-update-slice_fusion.7
  69.5 1.9 bitcast_dynamic-update-slice_fusion.6
  71.4 1.9 bitcast_dynamic-update-slice_fusion.5
  73.4 0.9 bitcast_dynamic-update-slice_fusion.4
  74.3 0.0 copy-done.3
  74.3 0.9 bitcast_dynamic-update-slice_fusion.3
  75.1 0.9 bitcast_dynamic-update-slice_fusion.2
  76.0 1.9 bitcast_dynamic-update-slice_fusion.1
  77.9 0.0 collective-permute-done.6
  77.9 0.8 bitcast_dynamic-update-slice_fusion
  78.8 5.3 %gather_fusion = bf16[8,384,768]{2,1,0:T(8,128)(2,1)} fusion(bf16[8,384,768]{2,1,0:T(8,128)(2,1)} %bitcast_dynamic-update-slice_fusion, s32[1024]{0:T(1024)S(1)} %pad_clamp_fusion), kind=kCustom, calls=%fused_computation | custom fusion | bytes 9437216 | tf_op jit(solution)/shard_map/gather | solution.py:27
  84.1 0.0 copy-done
  84.1 3.8 %multiply_reduce_fusion = (f32[256]{0:T(256)S(1)}, f32[768,256]{1,0:T(8,128)S(1)}) fusion(bf16[3072,768]{1,0:T(8,128)(2,1)} %bitcast.85, bf16[1,256,3072]{2,1,0:T(8,128)(2,1)S(1)} %copy-done), kind=kOutput, calls=%fused_computation.47 | convolution fusion | flops 1208352512 | bytes 7078912 | tf_op jit(solution)/shard_map/dot_general | solution.py:55
  87.9 0.1 bitcast_convert_fusion
  88.0 0.0 all-gather.3.cloned.1.call-done
  88.0 3.8 %fusion.28 = (f32[256]{0:T(256)S(1)}, f32[256,768]{0,1:T(8,128)S(1)}) fusion(f32[768,256]{1,0:T(8,128)S(1)} %get-tuple-element.14, f32[256]{0:T(256)S(1)} %add_rsqrt_fusion, bf16[1024,768]{1,0:T(8,128)(2,1)} %all-gather.3.cloned.1.call-done, bf16[256,768]{0,1:T(8,128)(2,1)S(1)} %bitcast_convert_fusion, f32[]{:T(128)} %bitcast.81, f32[]{:T(128)} %bitcast.72, ...), kind=kOutput, calls=%fused_computation.43 | convolution fusion | flops 809041664 | bytes 3546120 | tf_op jit(solution)/shard_map/dot_general | solution.py:102
  91.8 5.1 %convolution_bitcast_fusion = f32[3072,768]{0,1:T(8,128)} fusion(bf16[1,256,3072]{2,1,0:T(8,128)(2,1)S(1)} %copy-done, f32[256,768]{0,1:T(8,128)S(1)} %get-tuple-element.19, f32[768,256]{1,0:T(8,128)S(1)} %get-tuple-element.14, f32[256]{0:T(256)S(1)} %get-tuple-element.18, f32[256]{0:T(256)S(1)} %add_rsqrt_fusion), kind=kOutput, calls=%fused_computation.1 | convolution fusion | flops 1208942592 | bytes 12584960 | tf_op jit(solution)/shard_map/dot_general | solution.py:118
  96.9 9.6 %copy.16 = f32[3072,768]{1,0:T(8,128)} copy(f32[3072,768]{0,1:T(8,128)} %convolution_bitcast_fusion) | data formatting | bytes 18874368
  106.5 0.0 copy-start.1
  106.5 0.0 copy-start.4
  106.5 0.0 reduce-scatter.4.cloned.1.call-update
  106.5 1.5 collective-permute-start.7
  108.0 10.3 %collective-permute-done.7 = bf16[256,768]{0,1:T(8,128)(2,1)S(1)} collective-permute-done((bf16[256,768]{0,1:T(8,128)(2,1)S(1)}, bf16[256,768]{0,1:T(8,128)(2,1)S(1)}, u32[]{:S(2)}, u32[]{:S(2)}) %collective-permute-start.7) | collective-permute-done | bytes 393248 | tf_op jit(solution)/shard_map/ppermute | solution.py:34
  118.3 0.6 collective-permute-start.8
  118.9 0.0 copy-done.1
  118.9 0.3 fusion.12
  119.2 10.0 %collective-permute-done.8 = bf16[256,768]{0,1:T(8,128)(2,1)S(1)} collective-permute-done((bf16[256,768]{0,1:T(8,128)(2,1)S(1)}, bf16[256,768]{0,1:T(8,128)(2,1)S(1)}, u32[]{:S(2)}, u32[]{:S(2)}) %collective-permute-start.8) | collective-permute-done | bytes 393248 | tf_op jit(solution)/shard_map/ppermute | solution.py:34
  129.2 0.0 collective-permute-start.9
  129.2 0.0 copy-done.4
  129.2 0.4 fusion.83
  129.7 0.3 fusion.14
  130.0 9.2 %collective-permute-done.9 = bf16[256,768]{0,1:T(8,128)(2,1)S(1)} collective-permute-done((bf16[256,768]{0,1:T(8,128)(2,1)S(1)}, bf16[256,768]{0,1:T(8,128)(2,1)S(1)}, u32[]{:S(2)}, u32[]{:S(2)}) %collective-permute-start.9) | collective-permute-done | bytes 393248 | tf_op jit(solution)/shard_map/ppermute | solution.py:34
  139.1 0.3 fusion.15
  139.5 0.0 copy-start.2
  139.5 1.0 fusion.76
  140.5 0.6 add_add_fusion
  141.0 0.5 convolution_add_fusion.2
  141.5 0.5 convolution_add_fusion.1
  142.0 0.0 copy-done.2
  142.0 0.5 fusion.23
  142.5 1.0 fusion.39
  143.5 98.9 %reduce-scatter.4.cloned.1.call-done = f32[96,768]{1,0:T(8,128)} async-done(((f32[3072,768]{1,0:T(8,128)}), f32[96,768]{1,0:T(8,128)}) %reduce-scatter.4.cloned.1.call-update) | async-done | bytes 294928
  (6 shorter events, 0.0 us)
Async XLA Ops:
  7.2 77.0 %copy-start = (bf16[1,256,3072]{2,1,0:T(8,128)(2,1)S(1)}, bf16[1,256,3072]{2,1,0:T(8,128)(2,1)}, u32[]{:S(2)}) copy-start(bf16[1,256,3072]{2,1,0:T(8,128)(2,1)} %param.7) | copy-start | bytes 4718596
  7.2 67.1 %copy-start.3 = (bf16[384,768]{1,0:T(8,128)(2,1)S(1)}, bf16[384,768]{1,0:T(8,128)(2,1)}, u32[]{:S(2)}) copy-start(bf16[384,768]{1,0:T(8,128)(2,1)} %param.8) | copy-start | bytes 1769476
  7.2 80.8 %all-gather.3.cloned.1.call-start = ((), (), s32[]{:S(2)}) async-start(), calls=%async_computation.1 | async-start | bytes 1966080 | tf_op jit(solution)/shard_map/all_gather | solution.py:98
  7.2 12.3 %collective-permute-start = (bf16[384,768]{1,0:T(8,128)(2,1)}, bf16[384,768]{1,0:T(8,128)(2,1)S(1)}, u32[]{:S(2)}, u32[]{:S(2)}) collective-permute-start(bf16[384,768]{1,0:T(8,128)(2,1)} %param.8), channel_id=1, source_target_pairs={{0,1},{1,2},{2,3},{3,4},{4,5},{5,6},{6,7},{7,0},{8,9},{9,10},{10,1... | collective-permute-start | bytes 1769480 | tf_op jit(solution)/shard_map/ppermute | solution.py:22
  19.6 16.6 %collective-permute-start.1 = (bf16[384,768]{1,0:T(8,128)(2,1)S(1)}, bf16[384,768]{1,0:T(8,128)(2,1)}, u32[]{:S(2)}, u32[]{:S(2)}) collective-permute-start(bf16[384,768]{1,0:T(8,128)(2,1)S(1)} %collective-permute-done), channel_id=1, source_target_pairs={{0,1},{1,2},{2,3},{3,4},{4,5},{5,6},{6,7},{7,0},{8,9},{9,10},{10,1... | collective-permute-start | bytes 1769480 | tf_op jit(solution)/shard_map/ppermute | solution.py:22
  19.6 17.8 %collective-permute-start.4 = (bf16[384,768]{1,0:T(8,128)(2,1)}, bf16[384,768]{1,0:T(8,128)(2,1)S(1)}, u32[]{:S(2)}, u32[]{:S(2)}) collective-permute-start(bf16[384,768]{1,0:T(8,128)(2,1)} %param.8), channel_id=1, source_target_pairs={{1,0},{2,1},{3,2},{4,3},{5,4},{6,5},{7,6},{0,7},{9,8},{10,9},{11,1... | collective-permute-start | bytes 1769480 | tf_op jit(solution)/shard_map/ppermute | solution.py:24
  36.2 17.4 %collective-permute-start.2 = (bf16[384,768]{1,0:T(8,128)(2,1)}, bf16[384,768]{1,0:T(8,128)(2,1)}, u32[]{:S(2)}, u32[]{:S(2)}) collective-permute-start(bf16[384,768]{1,0:T(8,128)(2,1)} %collective-permute-done.1), channel_id=1, source_target_pairs={{0,1},{1,2},{2,3},{3,4},{4,5},{5,6},{6,7},{7,0},{8,9},{9,10},{10,1... | collective-permute-start | bytes 1769480 | tf_op jit(solution)/shard_map/ppermute | solution.py:22
  37.3 28.4 %collective-permute-start.5 = (bf16[384,768]{1,0:T(8,128)(2,1)S(1)}, bf16[384,768]{1,0:T(8,128)(2,1)}, u32[]{:S(2)}, u32[]{:S(2)}) collective-permute-start(bf16[384,768]{1,0:T(8,128)(2,1)S(1)} %collective-permute-done.4), channel_id=1, source_target_pairs={{1,0},{2,1},{3,2},{4,3},{5,4},{6,5},{7,6},{0,7},{9,8},{10,9},{11,1... | collective-permute-start | bytes 1769480 | tf_op jit(solution)/shard_map/ppermute | solution.py:24
  53.6 14.0 %collective-permute-start.3 = (bf16[384,768]{1,0:T(8,128)(2,1)}, bf16[384,768]{1,0:T(8,128)(2,1)}, u32[]{:S(2)}, u32[]{:S(2)}) collective-permute-start(bf16[384,768]{1,0:T(8,128)(2,1)} %collective-permute-done.2), channel_id=1, source_target_pairs={{0,1},{1,2},{2,3},{3,4},{4,5},{5,6},{6,7},{7,0},{8,9},{9,10},{10,1... | collective-permute-start | bytes 1769480 | tf_op jit(solution)/shard_map/ppermute | solution.py:22
  55.5 186.8 %reduce-scatter.4.cloned.1.call-start = ((), (), s32[]{:S(2)}) async-start(), calls=%async_computation.2 | async-start | bytes 9732096
  65.7 12.2 %collective-permute-start.6 = (bf16[384,768]{1,0:T(8,128)(2,1)}, bf16[384,768]{1,0:T(8,128)(2,1)S(1)}, u32[]{:S(2)}, u32[]{:S(2)}) collective-permute-start(bf16[384,768]{1,0:T(8,128)(2,1)} %collective-permute-done.5), channel_id=1, source_target_pairs={{1,0},{2,1},{3,2},{4,3},{5,4},{6,5},{7,6},{0,7},{9,8},{10,9},{11,1... | collective-permute-start | bytes 1769480 | tf_op jit(solution)/shard_map/ppermute | solution.py:24
  106.5 12.4 %copy-start.1 = (bf16[256,768]{1,0:T(8,128)(2,1)S(1)}, bf16[256,768]{1,0:T(8,128)(2,1)}, u32[]{:S(2)}) copy-start(bf16[256,768]{1,0:T(8,128)(2,1)} %fusion.22) | copy-start | bytes 1179652
  106.5 22.7 %copy-start.4 = (s32[1,256]{1,0:T(1,128)S(1)}, s32[1,256]{1,0:T(1,128)}, u32[]{:S(2)}) copy-start(s32[1,256]{1,0:T(1,128)} %param.9) | copy-start | bytes 3076
  106.5 11.8 %collective-permute-start.7 = (bf16[256,768]{0,1:T(8,128)(2,1)S(1)}, bf16[256,768]{0,1:T(8,128)(2,1)S(1)}, u32[]{:S(2)}, u32[]{:S(2)}) collective-permute-start(bf16[256,768]{0,1:T(8,128)(2,1)S(1)} %bitcast_convert_fusion), channel_id=1, source_target_pairs={{0,8},{8,16},{16,24},{24,0},{1,9},{9,17},{17,25},{25,1},{2,10},{10... | collective-permute-start | bytes 1179656 | tf_op jit(solution)/shard_map/ppermute | solution.py:34
  118.3 10.9 %collective-permute-start.8 = (bf16[256,768]{0,1:T(8,128)(2,1)S(1)}, bf16[256,768]{0,1:T(8,128)(2,1)S(1)}, u32[]{:S(2)}, u32[]{:S(2)}) collective-permute-start(bf16[256,768]{0,1:T(8,128)(2,1)S(1)} %collective-permute-done.7), channel_id=1, source_target_pairs={{0,8},{8,16},{16,24},{24,0},{1,9},{9,17},{17,25},{25,1},{2,10},{10... | collective-permute-start | bytes 1179656 | tf_op jit(solution)/shard_map/ppermute | solution.py:34
  129.2 9.9 %collective-permute-start.9 = (bf16[256,768]{0,1:T(8,128)(2,1)S(1)}, bf16[256,768]{0,1:T(8,128)(2,1)S(1)}, u32[]{:S(2)}, u32[]{:S(2)}) collective-permute-start(bf16[256,768]{0,1:T(8,128)(2,1)S(1)} %collective-permute-done.8), channel_id=1, source_target_pairs={{0,8},{8,16},{16,24},{24,0},{1,9},{9,17},{17,25},{25,1},{2,10},{10... | collective-permute-start | bytes 1179656 | tf_op jit(solution)/shard_map/ppermute | solution.py:34
  139.5 2.5 copy-start.2
Sparse Core Ops, SparseCore 0:
  55.6 32.3 all-gather.2
  106.7 135.6 reduce-scatter.3
